TPU v7x, 32 devices: a whole 2x2x4 slice. The times are simulated.
32 devices in a mesh: grp: 8 (over y, x, core), rep: 4 (over z).
Axes of the slice: x: 2, y: 2, z: 4, core: 2. Of those that a mesh axis runs over, the one named last changes fastest.
Arguments:
- features: bfloat16 [4096, 256], P(('grp', 'rep')), may hold values from -0.0625 to 0.0625
- weight: bfloat16 [256, 256], replicated, may hold values from -0.375 to 0.375
- preact: bfloat16 [4096, 256], P(('grp', 'rep')), may hold values from -6 to 6
- grad_out: bfloat16 [4096, 256], P(('grp', 'rep')), may hold values from -1.5 to 1.5
- degree: int32 [4096], P(('grp', 'rep')), may hold values from 1 to 64
- tile_values: bfloat16 [256, 4, 128, 128], P(('grp', 'rep')), may hold values from 0 to 1
- tile_rows: int32 [256, 4], P(('grp', 'rep')), may hold values from -1 to 3, as said below
Outputs:
- input_grad: float32 [4096, 256], P(('grp', 'rep'))
- weight_grad: float32 [256, 256], replicated
Inputs may be any that keep to these rules, and one draw needn't show every extreme that they name: `tile_rows`: each of the 8 rows of one device (aligned blocks) has up to 4 live slots; in every such block some row has all 4 slots live.
All inputs are finite; a program needn't handle non-finite values.
Results may differ from a plain program's by a relative error of at most 0.013.
Values may be sent and summed in bfloat16 or wider, within the bound.
No kernel may reach another device: no remote copies, remote signals or barrier semaphores. Data moves between devices by JAX's collectives and lax.ppermute only.
A program may use at most 128 MiB of HBM per device.

v0:
```python
import jax
import jax.numpy as jnp
from jax import lax
from jax.sharding import PartitionSpec as P


def tile_masks(tile_rows):
    tile_live = tile_rows >= 0
    clipped = jnp.where(tile_live, tile_rows, 0)
    return (tile_live, clipped)


def per_device(features, weight, preact, grad_out, degree, tile_values, tile_rows):
    rows_here = features.shape[0]
    feature_width = features.shape[1]
    tile_edge = tile_values.shape[2]
    slot_count = tile_values.shape[1]
    row_tiles = lax.axis_size("rep") * rows_here // tile_edge
    inverse = lax.rsqrt(degree.astype(jnp.float32))[:, None]
    grad_pre = jnp.where(preact > 0, grad_out, jnp.zeros_like(grad_out))
    tile_live, clipped = tile_masks(tile_rows)
    scaled = (features.astype(jnp.float32) * inverse).astype(jnp.bfloat16)
    gathered = lax.all_gather(scaled, "grp", axis=0, tiled=True)
    columns = gathered.reshape(-1, tile_edge, feature_width)
    target = jnp.where(tile_live, tile_rows, row_tiles)
    partial_value = jnp.zeros((row_tiles + 1, tile_edge, feature_width), jnp.float32)
    for slot in range(slot_count):
        product = jnp.einsum(
            "cij,cjf->cif", tile_values[:, slot], columns, preferred_element_type=jnp.float32
        )
        partial_value = partial_value.at[target[:, slot]].add(product)
    partial_value = partial_value[:row_tiles]
    summed = lax.psum_scatter(
        partial_value.reshape(row_tiles * tile_edge, feature_width).astype(jnp.bfloat16),
        "rep",
        scatter_dimension=0,
        tiled=True,
    ).astype(jnp.float32)
    aggregated = (summed * inverse).astype(jnp.bfloat16)
    weight_local = lax.dot_general(
        aggregated, grad_pre, (((0,), (0,)), ((), ())), preferred_element_type=jnp.float32
    )
    projected = (
        lax.dot_general(
            grad_pre, weight, (((1,), (1,)), ((), ())), preferred_element_type=jnp.float32
        )
        * inverse
    ).astype(jnp.bfloat16)
    block_rows = lax.all_gather(projected, "rep", axis=0, tiled=True)
    blocks = block_rows.reshape(row_tiles, tile_edge, feature_width)
    picked = jnp.take(blocks, clipped, axis=0)
    picked = jnp.where(tile_live[:, :, None, None], picked, jnp.zeros_like(picked))
    result = jnp.einsum("csij,csif->cjf", tile_values, picked, preferred_element_type=jnp.float32)
    input_grad = (
        lax.psum_scatter(
            result.reshape(rows_here * lax.axis_size("grp"), feature_width),
            "grp",
            scatter_dimension=0,
            tiled=True,
        )
        * inverse
    )
    weight_grad = lax.psum(weight_local, ("grp", "rep"))
    return (input_grad, weight_grad)


def solution(mesh):
    return jax.shard_map(
        per_device,
        mesh=mesh,
        in_specs=(
            P(("grp", "rep"), None),
            P(),
            P(("grp", "rep"), None),
            P(("grp", "rep"), None),
            P(("grp", "rep")),
            P(("grp", "rep"), None, None, None),
            P(("grp", "rep"), None),
        ),
        out_specs=(P(("grp", "rep"), None), P()),
        check_vma=False,
    )
```

profile of v0, /device:TPU:0, one launch (start us, length us, event | category | flops | bytes accessed | tf_op | source)
XLA Modules:
  0.0 254.5 jit_solution(7141739193772190387)
XLA Ops:
  7.2 0.0 copy-start
  7.2 0.0 reduce-scatter.3.cloned.1.call-start
  7.2 0.7 broadcast_select_fusion
  7.9 0.7 broadcast_compare_fusion
  8.6 0.7 convert_rsqrt_fusion
  9.3 0.0 copy-done
  9.3 1.1 fusion.5
  10.4 15.6 %all_gather.6 = bf16[512,256]{1,0:T(8,128)(2,1)S(1)} all-gather(bf16[128,256]{1,0:T(8,128)(2,1)S(1)} %fusion.5), channel_id=1, replica_groups=mesh['grp'=8,'rep'=4] {'rep'}, dimensions={0}, use_global_device_ids=true | all-gather | bytes 327680 | tf_op jit(solution)/shard_map/all_gather | solution.py:49
  26.0 0.1 copy.27
  26.1 0.1 reshape.27
  26.2 0.1 copy.25
  26.3 0.7 copy.26
  26.9 0.0 copy-start.1
  26.9 0.7 gather_fusion
  27.6 0.5 copy-done.1
  28.1 0.0 copy-start.4
  28.1 2.4 fusion
  30.5 0.0 reduce-scatter.3.cloned.1.call-update
  30.5 0.0 reduce-scatter.5.cloned.1.call-start
  30.6 0.5 fusion.21
  31.1 37.1 %reduce-scatter.3.cloned.1.call-done = f32[128,256]{1,0:T(8,128)} async-done(((f32[1024,256]{1,0:T(8,128)}), f32[128,256]{1,0:T(8,128)}) %reduce-scatter.3.cloned.1.call-update) | async-done | bytes 131088 | tf_op jit(solution)/shard_map/reduce_scatter | solution.py:55
  68.2 0.0 copy-done.4
  68.3 1.6 multiply_convert_fusion.1
  69.9 9.8 %all_gather.7 = bf16[1024,256]{1,0:T(8,128)(2,1)S(1)} all-gather(bf16[128,256]{1,0:T(8,128)(2,1)S(1)} %get-tuple-element.10), channel_id=1, replica_groups=mesh['grp'=8,'rep'=4] {'grp'}, dimensions={0}, use_global_device_ids=true | all-gather | bytes 589824 | tf_op jit(solution)/shard_map/all_gather | solution.py:23
  79.7 1.4 convolution_bitcast_fusion.3
  81.1 0.3 convolution_bitcast_fusion.2
  81.4 0.3 convolution_bitcast_fusion.1
  81.8 1.3 convolution_bitcast_fusion
  83.1 2.6 %copy.31 = f32[8,128,256]{2,1,0:T(8,128)} copy(f32[8,128,256]{1,2,0:T(8,128)} %convolution_bitcast_fusion.3) | data formatting | bytes 2097152 | tf_op jit(solution)/shard_map/cij,cjf->cif/dot_general | solution.py:28
  85.6 1.4 copy.34
  87.0 0.0 copy-start.6
  87.0 0.3 copy.37
  87.3 0.3 copy.40
  87.7 0.0 copy-start.5
  87.7 0.0 copy-done.6
  87.7 2.5 scatter_fusion
  90.2 0.0 copy-done.5
  90.2 2.5 scatter_fusion.1
  92.7 1.3 scatter_fusion.2
  94.0 0.0 copy-start.2
  94.0 0.0 copy-start.3
  94.0 1.3 scatter_fusion.3
  95.4 0.7 slice.61
  96.1 0.0 reduce-scatter.5.cloned.1.call-update
  96.1 0.0 all-reduce.2.cloned.1.call-start
  96.2 19.8 %reduce-scatter.5.cloned.1.call-done = bf16[128,256]{1,0:T(8,128)(2,1)} async-done(((bf16[512,256]{1,0:T(8,128)(2,1)}), bf16[128,256]{1,0:T(8,128)(2,1)}) %reduce-scatter.5.cloned.1.call-update) | async-done | bytes 65552 | tf_op jit(solution)/shard_map/reduce_scatter | solution.py:33
  115.9 0.0 copy-done.2
  115.9 0.0 copy-done.3
  115.9 1.8 fusion.16
  117.8 0.0 all-reduce.2.cloned.1.call-update
  117.8 128.5 %all-reduce.2.cloned.1.call-done = f32[256,256]{1,0:T(8,128)} async-done(((f32[256,256]{1,0:T(8,128)}), f32[256,256]{1,0:T(8,128)}) %all-reduce.2.cloned.1.call-update) | async-done | bytes 262160 | tf_op jit(solution)/shard_map/psum | solution.py:63
  246.3 1.7 copy.56
  (2 shorter events, 0.1 us)
Async XLA Ops:
  7.2 2.1 copy-start
  7.2 61.1 %reduce-scatter.3.cloned.1.call-start = ((), (), s32[]{:S(2)}) async-start(), calls=%async_computation.2 | async-start | bytes 1179648 | tf_op jit(solution)/shard_map/reduce_scatter | solution.py:55
  26.9 1.2 copy-start.1
  28.1 40.1 %copy-start.4 = (bf16[128,256]{1,0:T(8,128)(2,1)S(1)}, bf16[128,256]{1,0:T(8,128)(2,1)}, u32[]{:S(2)}) copy-start(bf16[128,256]{1,0:T(8,128)(2,1)} %param.7) | copy-start | bytes 196612
  30.5 85.4 %reduce-scatter.5.cloned.1.call-start = ((), (), s32[]{:S(2)}) async-start(), calls=%async_computation.3 | async-start | bytes 327680 | tf_op jit(solution)/shard_map/reduce_scatter | solution.py:33
  87.0 0.8 copy-start.6
  87.7 2.5 %copy-start.5 = (s32[8]{0:T(128)S(1)}, s32[8]{0:T(128)}, u32[]{:S(2)}) copy-start(s32[8]{0:T(128)} %get-tuple-element.4) | copy-start | bytes 100
  94.0 21.9 %copy-start.2 = (bf16[128,256]{1,0:T(8,128)(2,1)S(1)}, bf16[128,256]{1,0:T(8,128)(2,1)}, u32[]{:S(2)}) copy-start(bf16[128,256]{1,0:T(8,128)(2,1)} %param.10) | copy-start | bytes 196612
  94.0 21.9 %copy-start.3 = (bf16[128,256]{1,0:T(8,128)(2,1)S(1)}, bf16[128,256]{1,0:T(8,128)(2,1)}, u32[]{:S(2)}) copy-start(bf16[128,256]{1,0:T(8,128)(2,1)} %param.9) | copy-start | bytes 196612
  96.1 150.1 %all-reduce.2.cloned.1.call-start = ((), (), s32[]{:S(2)}) async-start(), calls=%async_computation.4 | async-start | bytes 524288 | tf_op jit(solution)/shard_map/psum | solution.py:63
Sparse Core Ops, SparseCore 0:
  30.7 37.5 reduce-scatter.2
  96.3 19.6 reduce-scatter.4
  122.9 123.2 all-reduce.1
where the time goes:
time: 255 us; the launch traced here: 254 us
  waiting for transfers between devices  185 us (73%)
  blocking collectives  25.4 us (10%)
  between operations  13.9 us (5%)
  other arithmetic  11.8 us (5%)
  local copies, waits for them, and re-layouts  9.19 us (4%)
  matrix products  8.64 us (3%)
    psum x1, waiting for transfers between devices, per_device(): weight_grad = lax.psum(weight_local, ('grp', 'rep'))  128 us
    reduce_scatter x1, waiting for transfers between devices, per_device(): lax.psum_scatter(result.reshape(rows_here * lax.axis_size('grp'), feature...  37.1 us
    reduce_scatter x1, waiting for transfers between devices, per_device(): lax.psum_scatter(partial_value.reshape(row_tiles * tile_edge, feature_wid...  19.8 us
    all_gather x1, blocking collectives, per_device(): block_rows = lax.all_gather(projected, 'rep', axis=0, tiled=True)  15.6 us
    all_gather x1, blocking collectives, per_device(): gathered = lax.all_gather(scaled, 'grp', axis=0, tiled=True)  9.77 us
    scatter-add x4, other arithmetic, per_device(): partial_value = partial_value.at[target[:, slot]].add(product)  7.56 us
  transfers between devices with their start and end apart: 3, of which 3 were waited for; matrix products, arithmetic and copies ran while one was open for 0% of the time, Pallas kernels for 0%

commit v1 on v0

--- a/solution.py
+++ b/solution.py
@@ -20,7 +20,14 @@
     grad_pre = jnp.where(preact > 0, grad_out, jnp.zeros_like(grad_out))
     tile_live, clipped = tile_masks(tile_rows)
     scaled = (features.astype(jnp.float32) * inverse).astype(jnp.bfloat16)
-    gathered = lax.all_gather(scaled, "grp", axis=0, tiled=True)
+    ways, here, hop = (lax.axis_size("grp"), lax.axis_index("grp"), scaled.shape[0])
+    line, have = (scaled, 1)
+    while have < ways:
+        line = jnp.concatenate(
+            [line, lax.ppermute(line, "grp", [(d, (d - have) % ways) for d in range(ways)])], axis=0
+        )
+        have = 2 * have
+    gathered = jnp.roll(line, here * hop, axis=0)
     columns = gathered.reshape(-1, tile_edge, feature_width)
     target = jnp.where(tile_live, tile_rows, row_tiles)
     partial_value = jnp.zeros((row_tiles + 1, tile_edge, feature_width), jnp.float32)

time: 255 us -> 244 us (0.957)
  blocking collectives: 25.4 us -> 14.8 us
  starting transfers between devices: 0.12 us -> 4.94 us
  waiting for transfers between devices: 185 us -> 181 us
    reduce_scatter x1, waiting for transfers between devices: 19.8 us -> 2.76 us  [per_device(): lax.psum_scatter(partial_value.reshape(row_tiles * tile_edge, feature_wid...]
    ppermute x0 -> x3, waiting for transfers between devices: none -> 11.7 us  [per_device(): lax.ppermute(line, 'grp', [(d, (d - have) % ways) for d in range(ways)])]
    all_gather x1 -> x0, blocking collectives: 9.77 us -> none  [per_device(): gathered = lax.all_gather(scaled, 'grp', axis=0, tiled=True)]
    ppermute x0 -> x3, starting transfers between devices: none -> 4.82 us  [per_device(): lax.ppermute(line, 'grp', [(d, (d - have) % ways) for d in range(ways)])]
  transfers between devices with their start and end apart: 3 -> 6, of which waited for: 3 -> 6; matrix products, arithmetic and copies ran while one was open for 0% -> 4% of each run, Pallas kernels for 0% -> 0%
where the time goes in v1:
time: 244 us
  waiting for transfers between devices  181 us (74%)
  blocking collectives  14.8 us (6%)
  between operations  13.9 us (6%)
  other arithmetic  12.2 us (5%)
  local copies, waits for them, and re-layouts  8.74 us (4%)
  matrix products  7.91 us (3%)
  starting transfers between devices  4.94 us (2%)
    psum x1, waiting for transfers between devices, per_device(): weight_grad = lax.psum(weight_local, ('grp', 'rep'))  130 us
    reduce_scatter x1, waiting for transfers between devices, per_device(): lax.psum_scatter(result.reshape(rows_here * lax.axis_size('grp'), feature...  36.6 us
    all_gather x1, blocking collectives, per_device(): block_rows = lax.all_gather(projected, 'rep', axis=0, tiled=True)  14.8 us
    ppermute x3, waiting for transfers between devices, per_device(): lax.ppermute(line, 'grp', [(d, (d - have) % ways) for d in range(ways)])  11.7 us
    scatter-add x4, other arithmetic, per_device(): partial_value = partial_value.at[target[:, slot]].add(product)  7.56 us
  transfers between devices with their start and end apart: 6, of which 6 were waited for; matrix products, arithmetic and copies ran while one was open for 4% of the time, Pallas kernels for 0%

profile of v1, /device:TPU:0, one launch (start us, length us, event | category | flops | bytes accessed | tf_op | source)
XLA Modules:
  0.0 243.9 jit_solution(9214949316030021556)
XLA Ops:
  7.2 0.0 copy-start
  7.2 0.0 reduce-scatter.5.cloned.1.call-start
  7.2 0.7 convert_rsqrt_fusion
  7.9 0.9 constant_dynamic-update-slice_fusion.7
  8.8 0.0 copy-start.1
  8.9 3.4 %collective-permute-start = (bf16[128,256]{1,0:T(8,128)(2,1)S(1)}, bf16[128,256]{1,0:T(8,128)(2,1)S(1)}, u32[]{:S(2)}, u32[]{:S(2)}) collective-permute-start(bf16[128,256]{1,0:T(8,128)(2,1)S(1)} %get-tuple-element.3), channel_id=1, source_target_pairs={{0,28},{4,0},{8,4},{12,8},{16,12},{20,16},{24,20},{28,24},{1,29},{... | collective-permute-start | bytes 196616 | tf_op jit(solution)/shard_map/ppermute | solution.py:27
  12.2 0.0 copy-done
  12.2 1.1 fusion.5
  13.3 0.7 broadcast_select_fusion
  14.0 0.1 collective-permute-done
  14.2 0.6 collective-permute-start.1
  14.8 5.2 %collective-permute-done.1 = bf16[256,256]{1,0:T(8,128)(2,1)S(1)} collective-permute-done((bf16[256,256]{1,0:T(8,128)(2,1)S(1)}, bf16[256,256]{1,0:T(8,128)(2,1)S(1)}, u32[]{:S(2)}, u32[]{:S(2)}) %collective-permute-start.1) | collective-permute-done | bytes 131104 | tf_op jit(solution)/shard_map/ppermute | solution.py:27
  20.0 0.8 collective-permute-start.2
  20.8 0.7 broadcast_compare_fusion
  21.6 6.3 %collective-permute-done.2 = bf16[512,256]{1,0:T(8,128)(2,1)S(1)} collective-permute-done((bf16[512,256]{1,0:T(8,128)(2,1)S(1)}, bf16[512,256]{1,0:T(8,128)(2,1)S(1)}, u32[]{:S(2)}, u32[]{:S(2)}) %collective-permute-start.2) | collective-permute-done | bytes 262176 | tf_op jit(solution)/shard_map/ppermute | solution.py:27
  28.0 0.0 copy-done.1
  28.0 1.4 convolution_bitcast_fusion.3
  29.4 0.3 convolution_bitcast_fusion.2
  29.8 0.3 convolution_bitcast_fusion.1
  30.1 1.3 convolution_bitcast_fusion
  31.4 2.5 %copy.27 = f32[8,128,256]{2,1,0:T(8,128)} copy(f32[8,128,256]{1,2,0:T(8,128)} %convolution_bitcast_fusion.3) | data formatting | bytes 2097152 | tf_op jit(solution)/shard_map/cij,cjf->cif/dot_general | solution.py:35
  34.0 1.4 copy.30
  35.4 0.3 copy.33
  35.7 0.3 copy.36
  36.1 2.5 %scatter_fusion = f32[5,128,256]{2,1,0:T(8,128)S(1)} fusion(f32[5,128,256]{2,1,0:T(8,128)S(1)} %broadcast_in_dim.40, s32[8]{0:T(128)S(1)} %get-tuple-element.7, f32[8,128,256]{2,1,0:T(8,128)} %copy.27), kind=kCustom, calls=%fused_computation.1 | custom fusion | flops 262144 | bytes 3145760 | tf_op jit(solution)/shard_map/scatter-add | solution.py:38
  38.6 2.5 %scatter_fusion.1 = f32[5,128,256]{2,1,0:T(8,128)S(1)} fusion(f32[5,128,256]{2,1,0:T(8,128)S(1)} %scatter_fusion, s32[8]{0:T(128)S(1)} %get-tuple-element.6, f32[8,128,256]{2,1,0:T(8,128)} %copy.30), kind=kCustom, calls=%fused_computation.2 | custom fusion | flops 262144 | bytes 3145760 | tf_op jit(solution)/shard_map/scatter-add | solution.py:38
  41.0 1.3 scatter_fusion.2
  42.4 1.3 scatter_fusion.3
  43.7 0.7 slice.61
  44.4 0.0 reduce-scatter.5.cloned.1.call-update
  44.4 0.0 reduce-scatter.3.cloned.1.call-start
  44.5 14.8 %all_gather.3 = bf16[512,256]{1,0:T(8,128)(2,1)S(1)} all-gather(bf16[128,256]{1,0:T(8,128)(2,1)S(1)} %fusion.5), channel_id=1, replica_groups=mesh['grp'=8,'rep'=4] {'rep'}, dimensions={0}, use_global_device_ids=true | all-gather | bytes 327680 | tf_op jit(solution)/shard_map/all_gather | solution.py:56
  59.3 0.1 copy.23
  59.3 0.1 reshape.27
  59.4 0.1 copy.21
  59.5 0.1 copy.22
  59.6 0.0 copy-start.2
  59.6 0.7 gather_fusion
  60.3 0.5 copy-done.2
  60.9 0.0 copy-start.3
  60.9 0.0 copy-start.4
  60.9 1.6 fusion
  62.5 0.0 reduce-scatter.3.cloned.1.call-update
  62.5 0.0 all-reduce.2.cloned.1.call-start
  62.6 2.8 %reduce-scatter.5.cloned.1.call-done = bf16[128,256]{1,0:T(8,128)(2,1)} async-done(((bf16[512,256]{1,0:T(8,128)(2,1)}), bf16[128,256]{1,0:T(8,128)(2,1)}) %reduce-scatter.5.cloned.1.call-update) | async-done | bytes 65552 | tf_op jit(solution)/shard_map/reduce_scatter | solution.py:40
  65.3 0.0 copy-done.3
  65.3 0.0 copy-done.4
  65.3 1.8 fusion.16
  67.2 0.0 all-reduce.2.cloned.1.call-update
  67.2 36.6 %reduce-scatter.3.cloned.1.call-done = f32[128,256]{1,0:T(8,128)} async-done(((f32[1024,256]{1,0:T(8,128)}), f32[128,256]{1,0:T(8,128)}) %reduce-scatter.3.cloned.1.call-update) | async-done | bytes 131088 | tf_op jit(solution)/shard_map/reduce_scatter | solution.py:62
  103.7 1.6 broadcast_multiply_fusion
  105.4 130.3 %all-reduce.2.cloned.1.call-done = f32[256,256]{1,0:T(8,128)} async-done(((f32[256,256]{1,0:T(8,128)}), f32[256,256]{1,0:T(8,128)}) %all-reduce.2.cloned.1.call-update) | async-done | bytes 262160 | tf_op jit(solution)/shard_map/psum | solution.py:70
  235.7 1.7 copy.59
  (13 shorter events, 0.2 us)
Async XLA Ops:
  7.2 5.1 %copy-start = (bf16[256,256]{1,0:T(8,128)(2,1)S(1)}, bf16[256,256]{1,0:T(8,128)(2,1)}, u32[]{:S(2)}) copy-start(bf16[256,256]{1,0:T(8,128)(2,1)} %param.8) | copy-start | bytes 393220
  7.2 58.2 %reduce-scatter.5.cloned.1.call-start = ((), (), s32[]{:S(2)}) async-start(), calls=%async_computation.3 | async-start | bytes 327680 | tf_op jit(solution)/shard_map/reduce_scatter | solution.py:40
  8.8 19.2 %copy-start.1 = (bf16[8,4,128,128]{3,2,1,0:T(8,128)(2,1)S(1)}, bf16[8,4,128,128]{3,2,1,0:T(8,128)(2,1)}, u32[]{:S(2)}) copy-start(bf16[8,4,128,128]{3,2,1,0:T(8,128)(2,1)} %param.12) | copy-start | bytes 3145732
  8.9 5.3 %collective-permute-start = (bf16[128,256]{1,0:T(8,128)(2,1)S(1)}, bf16[128,256]{1,0:T(8,128)(2,1)S(1)}, u32[]{:S(2)}, u32[]{:S(2)}) collective-permute-start(bf16[128,256]{1,0:T(8,128)(2,1)S(1)} %get-tuple-element.3), channel_id=1, source_target_pairs={{0,28},{4,0},{8,4},{12,8},{16,12},{20,16},{24,20},{28,24},{1,29},{... | collective-permute-start | bytes 196616 | tf_op jit(solution)/shard_map/ppermute | solution.py:27
  14.2 5.8 %collective-permute-start.1 = (bf16[256,256]{1,0:T(8,128)(2,1)S(1)}, bf16[256,256]{1,0:T(8,128)(2,1)S(1)}, u32[]{:S(2)}, u32[]{:S(2)}) collective-permute-start(bf16[256,256]{1,0:T(8,128)(2,1)S(1)} %pad_maximum_fusion.1), channel_id=1, source_target_pairs={{0,24},{4,28},{8,0},{12,4},{16,8},{20,12},{24,16},{28,20},{1,25},{... | collective-permute-start | bytes 393224 | tf_op jit(solution)/shard_map/ppermute | solution.py:27
  20.0 7.9 %collective-permute-start.2 = (bf16[512,256]{1,0:T(8,128)(2,1)S(1)}, bf16[512,256]{1,0:T(8,128)(2,1)S(1)}, u32[]{:S(2)}, u32[]{:S(2)}) collective-permute-start(bf16[512,256]{1,0:T(8,128)(2,1)S(1)} %pad_maximum_fusion), channel_id=1, source_target_pairs={{0,16},{4,20},{8,24},{12,28},{16,0},{20,4},{24,8},{28,12},{1,17},{... | collective-permute-start | bytes 786440 | tf_op jit(solution)/shard_map/ppermute | solution.py:27
  44.4 59.3 %reduce-scatter.3.cloned.1.call-start = ((), (), s32[]{:S(2)}) async-start(), calls=%async_computation.2 | async-start | bytes 1179648 | tf_op jit(solution)/shard_map/reduce_scatter | solution.py:62
  59.6 1.2 copy-start.2
  60.9 4.5 %copy-start.3 = (bf16[128,256]{1,0:T(8,128)(2,1)S(1)}, bf16[128,256]{1,0:T(8,128)(2,1)}, u32[]{:S(2)}) copy-start(bf16[128,256]{1,0:T(8,128)(2,1)} %param.10) | copy-start | bytes 196612
  60.9 4.5 %copy-start.4 = (bf16[128,256]{1,0:T(8,128)(2,1)S(1)}, bf16[128,256]{1,0:T(8,128)(2,1)}, u32[]{:S(2)}) copy-start(bf16[128,256]{1,0:T(8,128)(2,1)} %param.9) | copy-start | bytes 196612
  62.5 173.2 %all-reduce.2.cloned.1.call-start = ((), (), s32[]{:S(2)}) async-start(), calls=%async_computation.4 | async-start | bytes 524288 | tf_op jit(solution)/shard_map/psum | solution.py:70
Sparse Core Ops, SparseCore 0:
  44.6 20.7 reduce-scatter.4
  68.8 34.8 reduce-scatter.2
  110.7 124.9 all-reduce.1
